TPU v7x, 256 devices: a whole 4x4x8 slice. The times are simulated.
256 devices in a mesh: req: 32 (over z, y_hi, core), tp: 8 (over x, y_lo).
Axes of the slice: x: 4, y: 4 (y_hi: 2, y_lo: 2; y = y_hi * 2 + y_lo), z: 8, core: 2. Of those that a mesh axis runs over, the one named last changes fastest.
Arguments:
- tokens: bfloat16 [16384, 1024], P(('req', 'tp')), may hold values from -6 to 6
- w_qkv: bfloat16 [1024, 3, 1024], P(None, None, 'tp'), may hold values from -0.1875 to 0.1875
- w_out: bfloat16 [1024, 1024], P('tp'), may hold values from -0.75 to 0.75
- w_up: bfloat16 [1024, 4096], P(None, 'tp'), may hold values from -0.1875 to 0.1875
- b_up: float32 [4096], P('tp'), may hold values from -4 to 4
- w_down: bfloat16 [4096, 1024], P('tp'), may hold values from -0.09375 to 0.09375
- b_down: float32 [1024], replicated, may hold values from -3 to 3
- ln1_gain: float32 [1024], replicated, may hold values from 0.5 to 1.5
- ln1_bias: float32 [1024], replicated, may hold values from -3 to 3
- ln2_gain: float32 [1024], replicated, may hold values from 0.5 to 1.5
- ln2_bias: float32 [1024], replicated, may hold values from -3 to 3
- kv_cache: bfloat16 [2, 32, 16384, 1024], P(None, None, 'req', 'tp'), may hold values from -122 to 122
- cache_len: int32 [32], replicated, may hold values from 0 to 16384, as said below
- span_len: int32 [32], replicated, may hold values from 1 to 512, as said below
Outputs:
- output: bfloat16 [16384, 1024], P(('req', 'tp'))
Inputs may be any that keep to these rules, and one draw needn't show every extreme that they name: The first cache_len[r] positions of request r hold its keys and values; some request has 16384. Slots from span_len[r] on are padding whose keys are not attended to; some request has 512.
All inputs are finite; a program needn't handle non-finite values.
Results may differ from a plain program's by a relative error of at most 0.015.
Values may be sent and summed in bfloat16 or wider, within the bound.
No kernel may reach another device: no remote copies, remote signals or barrier semaphores. Data moves between devices by JAX's collectives and lax.ppermute only.
A program may use at most 128 MiB of HBM per device.

v0:
```python
import jax
import jax.numpy as jnp
from jax import lax
from jax.sharding import PartitionSpec as P

HEAD_DIM = 64
BLOCK_GROUP = 4
masked_score = -1e30


def layer_norm(values, gain, bias):
    centre = jnp.mean(values, axis=-1, keepdims=True)
    centred = values - centre
    variance = jnp.mean(centred * centred, axis=-1, keepdims=True)
    return centred * lax.rsqrt(variance + 1e-05) * gain + bias


def partial_attention(queries, key_rows, value_rows, allowed):
    scores = jnp.einsum(
        "chd,nhd->hcn", queries, key_rows, preferred_element_type=jnp.float32
    ) * queries.shape[-1] ** (-0.5)
    scores = jnp.where(allowed[None], scores, masked_score)
    peaks = jnp.max(scores, axis=-1)
    weights = jnp.where(allowed[None], jnp.exp(scores - peaks[..., None]), 0.0).astype(jnp.bfloat16)
    weight_sums = jnp.sum(weights.astype(jnp.float32), axis=-1)
    blended = jnp.einsum("hcn,nhd->chd", weights, value_rows, preferred_element_type=jnp.float32)
    return (peaks.T, weight_sums.T, blended.reshape(blended.shape[0], -1))


def merge_axis(peaks, weight_sums, blended, axis):
    highest = jnp.max(peaks, axis=axis, keepdims=True)
    factors = jnp.exp(peaks - highest)
    sums_out = jnp.sum(factors * weight_sums, axis=axis)
    spread = jnp.repeat(factors, blended.shape[-1] // peaks.shape[-1], axis=-1)
    blend_out = jnp.sum(spread * blended, axis=axis)
    return (jnp.squeeze(highest, axis=axis), sums_out, blend_out)


def cache_partials(queries, keys, values, cached_count):
    total_blocks, block_width = (keys.shape[0], keys.shape[1])
    group = BLOCK_GROUP if total_blocks % BLOCK_GROUP == 0 else 1

    def single(one_keys, one_values, block):
        places = block * block_width + jnp.arange(block_width, dtype=jnp.int32)
        allowed = jnp.broadcast_to(
            (places < cached_count)[None, :], (queries.shape[0], block_width)
        )
        return partial_attention(queries, one_keys, one_values, allowed)

    def grouped(items):
        return jax.vmap(single)(*items)

    def regroup(member):
        return member.reshape((total_blocks // group, group) + member.shape[1:])

    results = lax.map(
        grouped,
        (regroup(keys), regroup(values), regroup(jnp.arange(total_blocks, dtype=jnp.int32))),
    )
    return tuple((member.reshape((total_blocks,) + member.shape[2:]) for member in results))


def shards(
    tokens,
    w_qkv,
    w_out,
    w_up,
    b_up,
    w_down,
    b_down,
    ln1_gain,
    ln1_bias,
    ln2_gain,
    ln2_bias,
    kv_cache,
    cache_len,
    span_len,
):
    width_here = w_qkv.shape[2]
    heads_here = width_here // HEAD_DIM
    where_req = lax.axis_index("req")
    own_cache = lax.all_to_all(kv_cache, "req", split_axis=1, concat_axis=1, tiled=True)
    span_rows = lax.all_gather(tokens, "tp", axis=0, tiled=True)
    flat_qkv = w_qkv.reshape(w_qkv.shape[0], 3 * width_here)
    heads_qkv = jnp.dot(span_rows, flat_qkv, preferred_element_type=jnp.float32).astype(
        jnp.bfloat16
    )
    span = heads_qkv.shape[0]
    local_shape = (span, heads_here, HEAD_DIM)
    queries = heads_qkv[:, :width_here].reshape(local_shape)
    fresh_keys = heads_qkv[:, width_here : 2 * width_here].reshape(local_shape)
    fresh_values = heads_qkv[:, 2 * width_here :].reshape(local_shape)
    full_out = lax.all_gather(w_out, "tp", axis=0, tiled=True)
    fresh_count = span_len[where_req]
    cached_count = cache_len[where_req]
    positions = jnp.arange(span, dtype=jnp.int32)
    allowed = (positions[None, :] <= positions[:, None]) & (positions[None, :] < fresh_count)
    fresh = partial_attention(queries, fresh_keys, fresh_values, allowed)
    total_blocks, block_width = (own_cache.shape[1], own_cache.shape[2])
    cached = own_cache.reshape(2, total_blocks, block_width, heads_here, HEAD_DIM)
    peaks, weight_sums, blended = cache_partials(queries, cached[0], cached[1], cached_count)
    peaks, weight_sums, blended = merge_axis(
        jnp.concatenate([fresh[0][None], peaks]),
        jnp.concatenate([fresh[1][None], weight_sums]),
        jnp.concatenate([fresh[2][None], blended]),
        0,
    )
    attention = (blended / jnp.repeat(weight_sums, HEAD_DIM, axis=-1)).astype(jnp.bfloat16)
    attention = lax.all_to_all(attention, "tp", split_axis=0, concat_axis=1, tiled=True)
    projected = jnp.dot(attention, full_out, preferred_element_type=jnp.float32)
    normed = layer_norm(tokens.astype(jnp.float32) + projected, ln1_gain, ln1_bias).astype(
        jnp.bfloat16
    )
    n_tp = lax.axis_size("tp")
    span_normed = lax.all_to_all(
        jnp.broadcast_to(normed[None], (n_tp,) + normed.shape),
        "tp",
        split_axis=0,
        concat_axis=0,
        tiled=True,
    ).reshape(-1, normed.shape[1])
    hidden = jax.nn.gelu(
        jnp.dot(span_normed, w_up, preferred_element_type=jnp.float32) + b_up, approximate=False
    ).astype(jnp.bfloat16)
    partial = jnp.dot(hidden, w_down, preferred_element_type=jnp.float32).astype(jnp.bfloat16)
    partial = lax.all_to_all(
        partial.reshape((n_tp, -1) + partial.shape[1:]),
        "tp",
        split_axis=0,
        concat_axis=0,
        tiled=True,
    )
    summed = jnp.sum(partial.astype(jnp.float32), axis=0) + b_down + normed.astype(jnp.float32)
    return layer_norm(summed, ln2_gain, ln2_bias).astype(jnp.bfloat16)


def solution(mesh):
    placed = (
        P(("req", "tp"), None),
        P(None, None, "tp"),
        P("tp", None),
        P(None, "tp"),
        P("tp"),
        P("tp", None),
        P(),
        P(),
        P(),
        P(),
        P(),
        P(None, None, "req", "tp"),
        P(),
        P(),
    )
    return jax.shard_map(
        shards, mesh=mesh, in_specs=placed, out_specs=P(("req", "tp"), None), check_vma=False
    )
```

profile of v0, /device:TPU:8, one launch (start us, length us, event | category | flops | bytes accessed | tf_op | source)
XLA Modules:
  0.0 363.8 jit_solution(2658030651955312103)
XLA Ops:
  6.5 12.1 %copy.29 = bf16[2,32,512,128]{2,3,0,1:T(8,128)(2,1)} copy(bf16[2,32,512,128]{3,2,1,0:T(8,128)(2,1)} %param.27) | data formatting | bytes 16777216 | tf_op args[11]
  18.6 10.9 %all-to-all-start = ((bf16[2,32,512,128]{2,3,0,1:T(8,128)(2,1)}), bf16[2,32,512,128]{2,3,0,1:T(8,128)(2,1)}, u32[]{:S(2)}, u32[]{:S(2)}) async-start(bf16[2,32,512,128]{2,3,0,1:T(8,128)(2,1)} %copy.29), calls=%async_computation | async-start | bytes 16777216 | tf_op jit(solution)/shard_map/all_to_all | solution.py:82
  33.3 64.3 %all-gather.3.cloned.1.call-done = bf16[512,1024]{1,0:T(8,128)(2,1)} async-done(((bf16[64,1024]{1,0:T(8,128)(2,1)}), bf16[512,1024]{1,0:T(8,128)(2,1)}) %all-gather.3.cloned.1.call-update) | async-done | bytes 1048592 | tf_op jit(solution)/shard_map/all_gather | solution.py:83
  101.5 111.0 %all-to-all-done = bf16[2,32,512,128]{2,3,0,1:T(8,128)(2,1)} async-done(((bf16[2,32,512,128]{2,3,0,1:T(8,128)(2,1)}), bf16[2,32,512,128]{2,3,0,1:T(8,128)(2,1)}, u32[]{:S(2)}, u32[]{:S(2)}) %all-to-all-start) | async-done | bytes 8388640 | tf_op jit(solution)/shard_map/all_to_all | solution.py:82
  212.5 5.9 %fusion.93 = (bf16[1,32,512,128]{2,3,0,1:T(8,128)(2,1)}, bf16[1,32,512,128]{2,3,0,1:T(8,128)(2,1)}) fusion(bf16[2,32,512,128]{2,3,0,1:T(8,128)(2,1)} %all-to-all-done), kind=kLoop, calls=%fused_computation.137 | loop fusion | bytes 16777216 | tf_op jit(solution)/shard_map/slice | solution.py:101
  218.4 74.6 %while.14 = (s32[]{:T(128)}, f32[8,4,512,2]{2,1,3,0:T(4,128)S(1)}, f32[8,4,512,2]{2,3,1,0:T(2,128)S(1)}, f32[8,4,512,128]{2,3,1,0:T(8,128)}, s32[8,4]{1,0:T(8,12...) while((s32[]{:T(128)}, f32[8,4,512,2]{2,1,3,0:T(4,128)S(1)}, ...), condition=%wide.region_4.5_spmd, body=%wide.region_1.4_spmd.sunk | while | flops 557838336 | bytes 29612216 | solution.py:56
  219.2 3.0 bitcast_reduce_fusion.2
  222.2 2.6 convert_reduce_fusion.4
  228.6 3.0 bitcast_reduce_fusion.2
  231.6 2.6 convert_reduce_fusion.4
  237.9 3.0 bitcast_reduce_fusion.2
  240.9 2.6 convert_reduce_fusion.4
  243.5 1.9 fusion.113
  247.2 3.0 bitcast_reduce_fusion.2
  250.2 2.6 convert_reduce_fusion.4
  252.8 1.9 fusion.113
  256.5 3.0 bitcast_reduce_fusion.2
  259.5 2.6 convert_reduce_fusion.4
  265.9 3.0 bitcast_reduce_fusion.2
  268.9 2.6 convert_reduce_fusion.4
  275.2 3.0 bitcast_reduce_fusion.2
  278.2 2.6 convert_reduce_fusion.4
  280.8 1.9 fusion.113
  284.5 3.0 bitcast_reduce_fusion.2
  287.5 2.6 convert_reduce_fusion.4
  293.3 4.1 %fusion.12 = f32[512,2,64]{0,2,1:T(8,128)S(1)} fusion(f32[32,512,2,64]{1,3,2,0:T(8,128)} %bitcast.103, f32[1,512,2,64]{1,3,2,0:T(8,128)S(1)} %convolution_bitcast_fusion, f32[33,512,2]{1,2,0:T(2,128)S(1)} %get-tuple-element.105), kind=kLoop, calls=%fused_computation.24 | loop fusion | flops 6422528 | bytes 9048064 | tf_op jit(solution)/shard_map/reduce_sum | solution.py:35
  298.5 10.8 %all-to-all-start.1 = ((bf16[8,64,128]{2,1,0:T(8,128)(2,1)}), bf16[8,64,128]{2,1,0:T(8,128)(2,1)S(1)}, u32[]{:S(2)}, u32[]{:S(2)}) async-start(bf16[8,64,128]{2,1,0:T(8,128)(2,1)} %copy.35), calls=%async_computation.1 | async-start | bytes 262144 | tf_op jit(solution)/shard_map/all_to_all | solution.py:109
  309.3 5.4 %all-to-all-done.1 = bf16[8,64,128]{2,1,0:T(8,128)(2,1)S(1)} async-done(((bf16[8,64,128]{2,1,0:T(8,128)(2,1)}), bf16[8,64,128]{2,1,0:T(8,128)(2,1)S(1)}, u32[]{:S(2)}, u32[]{:S(2)}) %all-to-all-start.1) | async-done | bytes 131104 | tf_op jit(solution)/shard_map/all_to_all | solution.py:109
  314.7 2.2 fusion.95
  317.4 17.2 %all_to_all.31 = bf16[8,64,1024]{2,1,0:T(8,128)(2,1)S(1)} all-to-all(bf16[8,64,1024]{2,1,0:T(8,128)(2,1)S(1)} %broadcast_in_dim.109), channel_id=1, replica_groups=mesh['req'=32,'tp'=8] {'tp'}, dimensions={0} | all-to-all | bytes 2097152 | tf_op jit(solution)/shard_map/all_to_all | solution.py:115
  334.6 4.6 %convolution_convert_fusion = bf16[512,1024]{1,0:T(8,128)(2,1)S(1)} fusion(bf16[512,1024]{1,0:T(8,128)(2,1)S(1)} %copy-done, bf16[512,1024]{1,0:T(8,128)(2,1)S(1)} %bitcast.107, bf16[1024,512]{1,0:T(8,128)(2,1)} %param.19, f32[512]{0:T(512)S(1)} %copy-done.8), kind=kOutput, calls=%fused_computation.31 | convolution fusion | flops 1091567616 | bytes 4196352 | tf_op jit(solution)/shard_map/dot_general | solution.py:125
  339.3 16.2 %all_to_all.32 = bf16[8,64,1024]{2,1,0:T(8,128)(2,1)S(1)} all-to-all(bf16[8,64,1024]{2,1,0:T(8,128)(2,1)S(1)} %bitcast.108), channel_id=1, replica_groups=mesh['req'=32,'tp'=8] {'tp'}, dimensions={0} | all-to-all | bytes 2097152 | tf_op jit(solution)/shard_map/all_to_all | solution.py:126
  (104 shorter events, 35.2 us)
Async XLA Ops:
  6.5 328.1 %copy-start = (bf16[512,1024]{1,0:T(8,128)(2,1)S(1)}, bf16[512,1024]{1,0:T(8,128)(2,1)}, u32[]{:S(2)}) copy-start(bf16[512,1024]{1,0:T(8,128)(2,1)} %param.21) | copy-start | bytes 3145732
  18.6 12.4 %copy-start.1 = (bf16[1024,3,128]{2,0,1:T(8,128)(2,1)S(1)}, bf16[1024,3,128]{2,0,1:T(8,128)(2,1)}, u32[]{:S(2)}) copy-start(bf16[1024,3,128]{2,0,1:T(8,128)(2,1)} %param.17) | copy-start | bytes 2359300
  18.6 12.7 %copy-start.9 = (s32[32]{0:T(128)S(1)}, s32[32]{0:T(128)}, u32[]{:S(2)}) copy-start(s32[32]{0:T(128)} %param.28) | copy-start | bytes 388
  18.6 13.3 %copy-start.10 = (s32[32]{0:T(128)S(1)}, s32[32]{0:T(128)}, u32[]{:S(2)}) copy-start(s32[32]{0:T(128)} %param.29) | copy-start | bytes 388
  18.6 193.9 %all-to-all-start = ((bf16[2,32,512,128]{2,3,0,1:T(8,128)(2,1)}), bf16[2,32,512,128]{2,3,0,1:T(8,128)(2,1)}, u32[]{:S(2)}, u32[]{:S(2)}) async-start(bf16[2,32,512,128]{2,3,0,1:T(8,128)(2,1)} %copy.29), calls=%async_computation | async-start | bytes 16777216 | tf_op jit(solution)/shard_map/all_to_all | solution.py:82
  29.5 68.2 %all-gather.3.cloned.1.call-start = ((), (), s32[]{:S(2)}) async-start(), calls=%async_computation.4 | async-start | bytes 1179648 | tf_op jit(solution)/shard_map/all_gather | solution.py:83
  30.2 279.1 %all-gather.5.cloned.1.call-start = ((), (), s32[]{:S(2)}) async-start(), calls=%async_computation.5 | async-start | bytes 2359296 | tf_op jit(solution)/shard_map/all_gather | solution.py:93
  293.3 21.4 %copy-start.2 = (bf16[64,1024]{1,0:T(8,128)(2,1)S(1)}, bf16[64,1024]{1,0:T(8,128)(2,1)}, u32[]{:S(2)}) copy-start(bf16[64,1024]{1,0:T(8,128)(2,1)} %param.16) | copy-start | bytes 393220
  297.4 19.7 %copy-start.3 = (f32[1024]{0:T(1024)S(1)}, f32[1024]{0:T(1024)}, u32[]{:S(2)}) copy-start(f32[1024]{0:T(1024)} %param.24) | copy-start | bytes 12292
  297.4 19.7 %copy-start.4 = (f32[1024]{0:T(1024)S(1)}, f32[1024]{0:T(1024)}, u32[]{:S(2)}) copy-start(f32[1024]{0:T(1024)} %param.23) | copy-start | bytes 12292
  297.4 37.2 %copy-start.8 = (f32[512]{0:T(512)S(1)}, f32[512]{0:T(512)}, u32[]{:S(2)}) copy-start(f32[512]{0:T(512)} %param.20) | copy-start | bytes 6148
  298.5 16.2 %all-to-all-start.1 = ((bf16[8,64,128]{2,1,0:T(8,128)(2,1)}), bf16[8,64,128]{2,1,0:T(8,128)(2,1)S(1)}, u32[]{:S(2)}, u32[]{:S(2)}) async-start(bf16[8,64,128]{2,1,0:T(8,128)(2,1)} %copy.35), calls=%async_computation.1 | async-start | bytes 262144 | tf_op jit(solution)/shard_map/all_to_all | solution.py:109
  334.6 21.1 %copy-start.5 = (f32[1024]{0:T(1024)S(1)}, f32[1024]{0:T(1024)}, u32[]{:S(2)}) copy-start(f32[1024]{0:T(1024)} %param.22) | copy-start | bytes 12292
  339.2 16.9 %copy-start.6 = (f32[1024]{0:T(1024)S(1)}, f32[1024]{0:T(1024)}, u32[]{:S(2)}) copy-start(f32[1024]{0:T(1024)} %param.26) | copy-start | bytes 12292
  339.3 16.9 %copy-start.7 = (f32[1024]{0:T(1024)S(1)}, f32[1024]{0:T(1024)}, u32[]{:S(2)}) copy-start(f32[1024]{0:T(1024)} %param.25) | copy-start | bytes 12292
Sparse Core Ops, SparseCore 0:
  32.1 65.5 all-gather.2
  99.4 98.0 all-gather.4
where the time goes:
time: 365 us; the launch traced here: 364 us
  waiting for transfers between devices  182 us (50%)
  matrix products  48.9 us (13%)
  other arithmetic  34.1 us (9%)
  blocking collectives  33.4 us (9%)
  local copies, waits for them, and re-layouts  29.6 us (8%)
  starting transfers between devices  21.7 us (6%)
  between operations  13.7 us (4%)
    all_to_all x1, waiting for transfers between devices, shards(): lax.all_to_all(kv_cache, 'req', split_axis=1, concat_axis=1, tiled=True)  111 us
    all_gather x1, waiting for transfers between devices, shards(): span_rows = lax.all_gather(tokens, 'tp', axis=0, tiled=True)  64.3 us
    dot_general x9, matrix products, partial_attention(): jnp.einsum('chd,nhd->hcn', queries, key_rows, preferred_element_type=jnp....  24.5 us
    reduce_sum x9, other arithmetic, partial_attention(): weight_sums = jnp.sum(weights.astype(jnp.float32), axis=-1)  21.2 us
    all_to_all x1, blocking collectives, shards(): lax.all_to_all(jnp.broadcast_to(normed[None], (n_tp,) + normed.shape), 't...  17.2 us
    all_to_all x1, blocking collectives, shards(): lax.all_to_all(partial.reshape((n_tp, -1) + partial.shape[1:]), 'tp', spl...  16.2 us
    dot_general x9, matrix products, partial_attention(): jnp.einsum('hcn,nhd->chd', weights, value_rows, preferred_element_type=jn...  15.8 us
    unnamed x24, local copies, waits for them, and re-layouts  12.4 us
  transfers between devices with their start and end apart: 4, of which 3 were waited for; matrix products, arithmetic and copies ran while one was open for 25% of the time, Pallas kernels for 0%

commit v1 on v0

--- a/solution.py
+++ b/solution.py
@@ -106,7 +106,9 @@
         0,
     )
     attention = (blended / jnp.repeat(weight_sums, HEAD_DIM, axis=-1)).astype(jnp.bfloat16)
-    attention = lax.all_to_all(attention, "tp", split_axis=0, concat_axis=1, tiled=True)
+    pieces = jnp.split(attention, lax.axis_size("tp"), axis=0)
+    arrived = lax.all_to_all(jnp.stack(pieces), "tp", 0, 0)
+    attention = jnp.concatenate(arrived, axis=1)
     projected = jnp.dot(attention, full_out, preferred_element_type=jnp.float32)
     normed = layer_norm(tokens.astype(jnp.float32) + projected, ln1_gain, ln1_bias).astype(
         jnp.bfloat16

time: 365 us -> 370 us (1.014)
  local copies, waits for them, and re-layouts: 29.6 us -> 34.3 us
    unnamed x24 -> x31, local copies, waits for them, and re-layouts: 12.4 us -> 16.6 us
  transfers between devices with their start and end apart: 4 -> 4, of which waited for: 3 -> 3; matrix products, arithmetic and copies ran while one was open for 25% -> 26% of each run, Pallas kernels for 0% -> 0%
where the time goes in v1:
time: 370 us; the launch traced here: 369 us
  waiting for transfers between devices  182 us (49%)
  matrix products  48.9 us (13%)
  local copies, waits for them, and re-layouts  34.3 us (9%)
  other arithmetic  34.1 us (9%)
  blocking collectives  33.4 us (9%)
  starting transfers between devices  21.7 us (6%)
  between operations  13.7 us (4%)
    all_to_all x1, waiting for transfers between devices, shards(): lax.all_to_all(kv_cache, 'req', split_axis=1, concat_axis=1, tiled=True)  111 us
    all_gather x1, waiting for transfers between devices, shards(): span_rows = lax.all_gather(tokens, 'tp', axis=0, tiled=True)  64.3 us
    dot_general x9, matrix products, partial_attention(): jnp.einsum('chd,nhd->hcn', queries, key_rows, preferred_element_type=jnp....  24.5 us
    reduce_sum x9, other arithmetic, partial_attention(): weight_sums = jnp.sum(weights.astype(jnp.float32), axis=-1)  21.2 us
    all_to_all x1, blocking collectives, shards(): lax.all_to_all(jnp.broadcast_to(normed[None], (n_tp,) + normed.shape), 't...  17.2 us
    unnamed x31, local copies, waits for them, and re-layouts  16.6 us
    all_to_all x1, blocking collectives, shards(): lax.all_to_all(partial.reshape((n_tp, -1) + partial.shape[1:]), 'tp', spl...  16.2 us
    dot_general x9, matrix products, partial_attention(): jnp.einsum('hcn,nhd->chd', weights, value_rows, preferred_element_type=jn...  15.8 us
  transfers between devices with their start and end apart: 4, of which 3 were waited for; matrix products, arithmetic and copies ran while one was open for 26% of the time, Pallas kernels for 0%

profile of v1, /device:TPU:8, one launch (start us, length us, event | category | flops | bytes accessed | tf_op | source)
XLA Modules:
  0.0 368.6 jit_solution(18010971147278018790)
XLA Ops:
  6.5 12.1 %copy.36 = bf16[2,32,512,128]{2,3,0,1:T(8,128)(2,1)} copy(bf16[2,32,512,128]{3,2,1,0:T(8,128)(2,1)} %param.27) | data formatting | bytes 16777216 | tf_op args[11]
  18.6 10.9 %all-to-all-start = ((bf16[2,32,512,128]{2,3,0,1:T(8,128)(2,1)}), bf16[2,32,512,128]{2,3,0,1:T(8,128)(2,1)}, u32[]{:S(2)}, u32[]{:S(2)}) async-start(bf16[2,32,512,128]{2,3,0,1:T(8,128)(2,1)} %copy.36), calls=%async_computation | async-start | bytes 16777216 | tf_op jit(solution)/shard_map/all_to_all | solution.py:82
  33.3 64.3 %all-gather.3.cloned.1.call-done = bf16[512,1024]{1,0:T(8,128)(2,1)} async-done(((bf16[64,1024]{1,0:T(8,128)(2,1)}), bf16[512,1024]{1,0:T(8,128)(2,1)}) %all-gather.3.cloned.1.call-update) | async-done | bytes 1048592 | tf_op jit(solution)/shard_map/all_gather | solution.py:83
  101.5 111.0 %all-to-all-done = bf16[2,32,512,128]{2,3,0,1:T(8,128)(2,1)} async-done(((bf16[2,32,512,128]{2,3,0,1:T(8,128)(2,1)}), bf16[2,32,512,128]{2,3,0,1:T(8,128)(2,1)}, u32[]{:S(2)}, u32[]{:S(2)}) %all-to-all-start) | async-done | bytes 8388640 | tf_op jit(solution)/shard_map/all_to_all | solution.py:82
  212.5 5.9 %fusion.93 = (bf16[1,32,512,128]{2,3,0,1:T(8,128)(2,1)}, bf16[1,32,512,128]{2,3,0,1:T(8,128)(2,1)}) fusion(bf16[2,32,512,128]{2,3,0,1:T(8,128)(2,1)} %all-to-all-done), kind=kLoop, calls=%fused_computation.145 | loop fusion | bytes 16777216 | tf_op jit(solution)/shard_map/slice | solution.py:101
  218.4 74.6 %while.14 = (s32[]{:T(128)}, f32[8,4,512,2]{2,1,3,0:T(4,128)S(1)}, f32[8,4,512,2]{2,3,1,0:T(2,128)S(1)}, f32[8,4,512,128]{2,3,1,0:T(8,128)}, s32[8,4]{1,0:T(8,12...) while((s32[]{:T(128)}, f32[8,4,512,2]{2,1,3,0:T(4,128)S(1)}, ...), condition=%wide.region_4.5_spmd, body=%wide.region_1.4_spmd.sunk | while | flops 557838336 | bytes 29612216 | solution.py:56
  219.2 3.0 bitcast_reduce_fusion.2
  222.2 2.6 convert_reduce_fusion.4
  228.6 3.0 bitcast_reduce_fusion.2
  231.6 2.6 convert_reduce_fusion.4
  237.9 3.0 bitcast_reduce_fusion.2
  240.9 2.6 convert_reduce_fusion.4
  243.5 1.9 fusion.114
  247.2 3.0 bitcast_reduce_fusion.2
  250.2 2.6 convert_reduce_fusion.4
  252.8 1.9 fusion.114
  256.5 3.0 bitcast_reduce_fusion.2
  259.5 2.6 convert_reduce_fusion.4
  265.9 3.0 bitcast_reduce_fusion.2
  268.9 2.6 convert_reduce_fusion.4
  275.2 3.0 bitcast_reduce_fusion.2
  278.2 2.6 convert_reduce_fusion.4
  280.8 1.9 fusion.114
  284.5 3.0 bitcast_reduce_fusion.2
  287.5 2.6 convert_reduce_fusion.4
  293.3 4.1 %fusion.12 = f32[512,2,64]{0,2,1:T(8,128)S(1)} fusion(f32[32,512,2,64]{1,3,2,0:T(8,128)} %bitcast.109, f32[1,512,2,64]{1,3,2,0:T(8,128)S(1)} %convolution_bitcast_fusion, f32[33,512,2]{1,2,0:T(2,128)S(1)} %get-tuple-element.114), kind=kLoop, calls=%fused_computation.24 | loop fusion | flops 6422528 | bytes 9048064 | tf_op jit(solution)/shard_map/reduce_sum | solution.py:35
  303.3 10.8 %all-to-all-start.1 = ((bf16[8,64,128]{2,1,0:T(8,128)(2,1)}), bf16[8,64,128]{2,1,0:T(8,128)(2,1)S(1)}, u32[]{:S(2)}, u32[]{:S(2)}) async-start(bf16[8,64,128]{2,1,0:T(8,128)(2,1)} %constant_dynamic-update-slice_fusion.1), calls=%async_computation.1 | async-start | bytes 262144 | tf_op jit(solution)/shard_map/all_to_all | solution.py:110
  314.1 5.4 %all-to-all-done.1 = bf16[8,64,128]{2,1,0:T(8,128)(2,1)S(1)} async-done(((bf16[8,64,128]{2,1,0:T(8,128)(2,1)}), bf16[8,64,128]{2,1,0:T(8,128)(2,1)S(1)}, u32[]{:S(2)}, u32[]{:S(2)}) %all-to-all-start.1) | async-done | bytes 131104 | tf_op jit(solution)/shard_map/all_to_all | solution.py:110
  319.5 2.2 fusion.96
  322.2 17.2 %all_to_all.20 = bf16[8,64,1024]{2,1,0:T(8,128)(2,1)S(1)} all-to-all(bf16[8,64,1024]{2,1,0:T(8,128)(2,1)S(1)} %broadcast_in_dim.109), channel_id=1, replica_groups=mesh['req'=32,'tp'=8] {'tp'}, dimensions={0} | all-to-all | bytes 2097152 | tf_op jit(solution)/shard_map/all_to_all | solution.py:117
  339.4 4.6 %convolution_convert_fusion = bf16[512,1024]{1,0:T(8,128)(2,1)S(1)} fusion(bf16[512,1024]{1,0:T(8,128)(2,1)S(1)} %copy-done, bf16[512,1024]{1,0:T(8,128)(2,1)S(1)} %bitcast.113, bf16[1024,512]{1,0:T(8,128)(2,1)} %param.19, f32[512]{0:T(512)S(1)} %copy-done.8), kind=kOutput, calls=%fused_computation.31 | convolution fusion | flops 1091567616 | bytes 4196352 | tf_op jit(solution)/shard_map/dot_general | solution.py:127
  344.0 16.2 %all_to_all.21 = bf16[8,64,1024]{2,1,0:T(8,128)(2,1)S(1)} all-to-all(bf16[8,64,1024]{2,1,0:T(8,128)(2,1)S(1)} %bitcast.114), channel_id=1, replica_groups=mesh['req'=32,'tp'=8] {'tp'}, dimensions={0} | all-to-all | bytes 2097152 | tf_op jit(solution)/shard_map/all_to_all | solution.py:128
  (119 shorter events, 39.9 us)
Async XLA Ops:
  6.5 332.8 %copy-start = (bf16[512,1024]{1,0:T(8,128)(2,1)S(1)}, bf16[512,1024]{1,0:T(8,128)(2,1)}, u32[]{:S(2)}) copy-start(bf16[512,1024]{1,0:T(8,128)(2,1)} %param.21) | copy-start | bytes 3145732
  18.6 12.4 %copy-start.1 = (bf16[1024,3,128]{2,0,1:T(8,128)(2,1)S(1)}, bf16[1024,3,128]{2,0,1:T(8,128)(2,1)}, u32[]{:S(2)}) copy-start(bf16[1024,3,128]{2,0,1:T(8,128)(2,1)} %param.17) | copy-start | bytes 2359300
  18.6 12.7 %copy-start.9 = (s32[32]{0:T(128)S(1)}, s32[32]{0:T(128)}, u32[]{:S(2)}) copy-start(s32[32]{0:T(128)} %param.28) | copy-start | bytes 388
  18.6 13.3 %copy-start.10 = (s32[32]{0:T(128)S(1)}, s32[32]{0:T(128)}, u32[]{:S(2)}) copy-start(s32[32]{0:T(128)} %param.29) | copy-start | bytes 388
  18.6 193.9 %all-to-all-start = ((bf16[2,32,512,128]{2,3,0,1:T(8,128)(2,1)}), bf16[2,32,512,128]{2,3,0,1:T(8,128)(2,1)}, u32[]{:S(2)}, u32[]{:S(2)}) async-start(bf16[2,32,512,128]{2,3,0,1:T(8,128)(2,1)} %copy.36), calls=%async_computation | async-start | bytes 16777216 | tf_op jit(solution)/shard_map/all_to_all | solution.py:82
  29.5 68.2 %all-gather.3.cloned.1.call-start = ((), (), s32[]{:S(2)}) async-start(), calls=%async_computation.4 | async-start | bytes 1179648 | tf_op jit(solution)/shard_map/all_gather | solution.py:83
  30.2 283.9 %all-gather.5.cloned.1.call-start = ((), (), s32[]{:S(2)}) async-start(), calls=%async_computation.5 | async-start | bytes 2359296 | tf_op jit(solution)/shard_map/all_gather | solution.py:93
  293.3 26.2 %copy-start.2 = (bf16[64,1024]{1,0:T(8,128)(2,1)S(1)}, bf16[64,1024]{1,0:T(8,128)(2,1)}, u32[]{:S(2)}) copy-start(bf16[64,1024]{1,0:T(8,128)(2,1)} %param.16) | copy-start | bytes 393220
  297.4 24.5 %copy-start.3 = (f32[1024]{0:T(1024)S(1)}, f32[1024]{0:T(1024)}, u32[]{:S(2)}) copy-start(f32[1024]{0:T(1024)} %param.24) | copy-start | bytes 12292
  297.4 24.5 %copy-start.4 = (f32[1024]{0:T(1024)S(1)}, f32[1024]{0:T(1024)}, u32[]{:S(2)}) copy-start(f32[1024]{0:T(1024)} %param.23) | copy-start | bytes 12292
  297.4 41.9 %copy-start.8 = (f32[512]{0:T(512)S(1)}, f32[512]{0:T(512)}, u32[]{:S(2)}) copy-start(f32[512]{0:T(512)} %param.20) | copy-start | bytes 6148
  303.3 16.2 %all-to-all-start.1 = ((bf16[8,64,128]{2,1,0:T(8,128)(2,1)}), bf16[8,64,128]{2,1,0:T(8,128)(2,1)S(1)}, u32[]{:S(2)}, u32[]{:S(2)}) async-start(bf16[8,64,128]{2,1,0:T(8,128)(2,1)} %constant_dynamic-update-slice_fusion.1), calls=%async_computation.1 | async-start | bytes 262144 | tf_op jit(solution)/shard_map/all_to_all | solution.py:110
  339.4 21.1 %copy-start.5 = (f32[1024]{0:T(1024)S(1)}, f32[1024]{0:T(1024)}, u32[]{:S(2)}) copy-start(f32[1024]{0:T(1024)} %param.22) | copy-start | bytes 12292
  344.0 16.9 %copy-start.6 = (f32[1024]{0:T(1024)S(1)}, f32[1024]{0:T(1024)}, u32[]{:S(2)}) copy-start(f32[1024]{0:T(1024)} %param.26) | copy-start | bytes 12292
  344.0 16.9 %copy-start.7 = (f32[1024]{0:T(1024)S(1)}, f32[1024]{0:T(1024)}, u32[]{:S(2)}) copy-start(f32[1024]{0:T(1024)} %param.25) | copy-start | bytes 12292
Sparse Core Ops, SparseCore 0:
  32.1 65.5 all-gather.2
  99.4 98.0 all-gather.4
